TPU v7x, 32 devices: a whole 2x2x4 slice. The times are simulated.
32 devices in a mesh: dp: 8 (over z, y), tensor: 4 (over x, core).
Axes of the slice: x: 2, y: 2, z: 4, core: 2. Of those that a mesh axis runs over, the one named last changes fastest.
Arguments:
- tokens: bfloat16 [8, 1024, 1536], P('dp'), may hold values from -6 to 6
- piece_starts: int32 [8, 2], P('dp'), may hold values from -1 to 768, as said below
- attn_gain: bfloat16 [1536], P('dp'), may hold values from 0.5 to 1.5
- w_query: bfloat16 [1536, 1536], P('dp', 'tensor'), may hold values from -0.15625 to 0.15625
- w_key: bfloat16 [1536, 1536], P('dp', 'tensor'), may hold values from -0.15625 to 0.15625
- w_value: bfloat16 [1536, 1536], P('dp', 'tensor'), may hold values from -0.15625 to 0.15625
- w_outgate: bfloat16 [1536, 1536], P('dp', 'tensor'), may hold values from -0.15625 to 0.15625
- w_forget: bfloat16 [1536, 24], P('dp', 'tensor'), may hold values from -0.3125 to 0.3125
- forget_bias: float32 [24], P('tensor'), may hold values from 2 to 8
- w_output: bfloat16 [1536, 1536], P('tensor', 'dp'), may hold values from -0.4375 to 0.4375
- ffn_gain: bfloat16 [1536], P('dp'), may hold values from 0.5 to 1.5
- w_gate: bfloat16 [1536, 4096], P('dp', 'tensor'), may hold values from -0.15625 to 0.15625
- w_up: bfloat16 [1536, 4096], P('dp', 'tensor'), may hold values from -0.15625 to 0.15625
- w_down: bfloat16 [4096, 1536], P('tensor', 'dp'), may hold values from -0.09375 to 0.09375
- cotangent: bfloat16 [8, 1024, 1536], P('dp'), may hold values from -6 to 6
Outputs:
- output: bfloat16 [8, 1024, 1536], P('dp')
- tokens_grad: bfloat16 [8, 1024, 1536], P('dp')
- attn_gain_grad: float32 [1536], P('dp')
- w_query_grad: float32 [1536, 1536], P('dp', 'tensor')
- w_key_grad: float32 [1536, 1536], P('dp', 'tensor')
- w_value_grad: float32 [1536, 1536], P('dp', 'tensor')
- w_outgate_grad: float32 [1536, 1536], P('dp', 'tensor')
- w_forget_grad: float32 [1536, 24], P('dp', 'tensor')
- forget_bias_grad: float32 [24], P('tensor')
- w_output_grad: float32 [1536, 1536], P('tensor', 'dp')
- ffn_gain_grad: float32 [1536], P('dp')
- w_gate_grad: float32 [1536, 4096], P('dp', 'tensor')
- w_up_grad: float32 [1536, 4096], P('dp', 'tensor')
- w_down_grad: float32 [4096, 1536], P('tensor', 'dp')
Inputs may be any that keep to these rules, and one draw needn't show every extreme that they name: `piece_starts`: slot k of a sequence's row holds -1 (no piece) or a start in [k * 512, (k + 1) * 512 - 256], so pieces never intersect; the number of pieces differs between sequences.
All inputs are finite; a program needn't handle non-finite values.
Results may differ from a plain program's by a relative error of at most 0.025.
Values may be sent and summed in bfloat16 or wider, within the bound.
No kernel may reach another device: no remote copies, remote signals or barrier semaphores. Data moves between devices by JAX's collectives and lax.ppermute only.
A program may use at most 256 MiB of HBM per device.

v0:
```python
import jax
import jax.numpy as jnp
from jax import lax
from jax.sharding import PartitionSpec as P

PIECE = 256
epsilon = 1e-06
masked_value = -1e30


def project(left, right):
    return jnp.dot(left, right, preferred_element_type=jnp.float32)


def contract_rows(left, right):
    return lax.dot_general(
        left, right, (((0,), (0,)), ((), ())), preferred_element_type=jnp.float32
    )


def contract_cols(left, right):
    return lax.dot_general(
        left, right, (((1,), (1,)), ((), ())), preferred_element_type=jnp.float32
    )


def allowed_pairs(starts, length):
    places = jnp.arange(length, dtype=jnp.int32)
    inside = (
        (starts[:, None] >= 0)
        & (places[None, :] >= starts[:, None])
        & (places[None, :] < starts[:, None] + PIECE)
    )
    labels = jnp.sum(
        jnp.where(inside, jnp.arange(1, starts.shape[0] + 1, dtype=jnp.int32)[:, None], 0), axis=0
    )
    same = (labels[:, None] == labels[None, :]) & (labels[:, None] > 0)
    return (places[None, :] <= places[:, None]) | same


def block_scores(query_rows, key_all, decay, allowed_rows, first_row):
    count = query_rows.shape[0]
    raw = jnp.einsum(
        "qhd,khd->hqk", query_rows, key_all, preferred_element_type=jnp.float32
    ) * query_rows.shape[-1] ** (-0.5)
    apart = (
        lax.slice_in_dim(decay, first_row, first_row + count, axis=1)[:, :, None]
        - decay[:, None, :]
    )
    return (jnp.where(allowed_rows[None], raw - jnp.abs(apart), masked_value), apart)


def attend_forward(items):
    query_all, key_all, value_all, log_forget, starts = items
    length = query_all.shape[0]
    block_rows = min(512, length)
    decay = jnp.cumsum(log_forget, axis=0).T
    allowed = allowed_pairs(starts, length)
    results = []
    normalizers = []
    for first_row in range(0, length, block_rows):
        scores, apart = block_scores(
            query_all[first_row : first_row + block_rows],
            key_all,
            decay,
            allowed[first_row : first_row + block_rows],
            first_row,
        )
        largest = jnp.max(scores, axis=-1, keepdims=True)
        weights = jnp.exp(scores - largest)
        denominator = jnp.sum(weights, axis=-1, keepdims=True)
        chances = (weights / denominator).astype(jnp.bfloat16)
        results.append(
            jnp.einsum("hqk,khd->qhd", chances, value_all, preferred_element_type=jnp.float32)
        )
        normalizers.append(largest + jnp.log(denominator))
    return (jnp.concatenate(results, axis=0), jnp.concatenate(normalizers, axis=1))


def attend_backward(items):
    query_all, key_all, value_all, log_forget, starts, attended, normalizer, grad_out = items
    length = query_all.shape[0]
    block_rows = min(512, length)
    scale = query_all.shape[-1] ** (-0.5)
    decay = jnp.cumsum(log_forget, axis=0).T
    allowed = allowed_pairs(starts, length)
    grad_key = jnp.zeros(key_all.shape, jnp.float32)
    grad_value = jnp.zeros(value_all.shape, jnp.float32)
    grad_decay = jnp.zeros(decay.shape, jnp.float32)
    query_parts = []
    row_parts = []
    for first_row in range(0, length, block_rows):
        query_rows = query_all[first_row : first_row + block_rows]
        out_rows = grad_out[first_row : first_row + block_rows]
        scores, apart = block_scores(
            query_rows, key_all, decay, allowed[first_row : first_row + block_rows], first_row
        )
        chances = jnp.exp(scores - normalizer[:, first_row : first_row + block_rows])
        grad_chance = jnp.einsum(
            "qhd,khd->hqk", out_rows, value_all, preferred_element_type=jnp.float32
        )
        offset = jnp.sum(
            out_rows.astype(jnp.float32) * attended[first_row : first_row + block_rows], axis=-1
        ).T[:, :, None]
        grad_score = chances * (grad_chance - offset)
        grad_rounded = grad_score.astype(jnp.bfloat16)
        grad_value = grad_value + jnp.einsum(
            "hqk,qhd->khd",
            chances.astype(jnp.bfloat16),
            out_rows,
            preferred_element_type=jnp.float32,
        )
        grad_key = (
            grad_key
            + jnp.einsum(
                "hqk,qhd->khd", grad_rounded, query_rows, preferred_element_type=jnp.float32
            )
            * scale
        )
        query_parts.append(
            jnp.einsum("hqk,khd->qhd", grad_rounded, key_all, preferred_element_type=jnp.float32)
            * scale
        )
        signed = grad_score * jnp.sign(apart)
        grad_decay = grad_decay + jnp.sum(signed, axis=1)
        row_parts.append(-jnp.sum(signed, axis=-1))
    grad_decay = grad_decay + jnp.concatenate(row_parts, axis=1)
    grad_log = jnp.flip(jnp.cumsum(jnp.flip(grad_decay, axis=1), axis=1), axis=1).T
    grad_query = jnp.concatenate(query_parts, axis=0)
    return (
        grad_query.astype(jnp.bfloat16),
        grad_key.astype(jnp.bfloat16),
        grad_value.astype(jnp.bfloat16),
        grad_log,
    )


def on_device(
    tokens,
    piece_starts,
    attn_gain,
    w_query,
    w_key,
    w_value,
    w_outgate,
    w_forget,
    forget_bias,
    w_output,
    ffn_gain,
    w_gate,
    w_up,
    w_down,
    cotangent,
):
    sequences, length, width = tokens.shape
    heads_here = w_forget.shape[1]
    share_width = w_query.shape[1]
    head_size = share_width // heads_here
    row_count = sequences * length
    block = w_query.shape[0]
    units = w_gate.shape[1]

    def head_view(values):
        return values.reshape(sequences, length, heads_here, head_size)

    attn_local = jnp.concatenate(
        [w_query, w_key, w_value, w_outgate, w_output.T, w_forget, attn_gain[:, None]], axis=1
    )
    attn_full = lax.all_gather(attn_local, "dp", axis=0, tiled=True)
    joined = attn_full[:, : 4 * share_width]
    output_t = attn_full[:, 4 * share_width : 5 * share_width]
    forget_w = attn_full[:, 5 * share_width : 5 * share_width + heads_here]
    gain_one = attn_full[:, 5 * share_width + heads_here].astype(jnp.float32)
    ffn_local = jnp.concatenate([w_gate, w_up, w_down.T, ffn_gain[:, None]], axis=1)
    ffn_full = lax.all_gather(ffn_local, "dp", axis=0, tiled=True)
    gate_up_w = ffn_full[:, : 2 * units]
    down_t = ffn_full[:, 2 * units : 3 * units]
    gain_two = ffn_full[:, 3 * units].astype(jnp.float32)
    inputs = tokens.reshape(row_count, width).astype(jnp.float32)
    scale_one = lax.rsqrt(jnp.mean(inputs * inputs, axis=-1, keepdims=True) + epsilon)
    unit_one = inputs * scale_one
    normed = (unit_one * gain_one).astype(jnp.bfloat16)
    projected = project(normed, joined)
    query_all = head_view(projected[:, :share_width].astype(jnp.bfloat16))
    key_all = head_view(projected[:, share_width : 2 * share_width].astype(jnp.bfloat16))
    value_all = head_view(projected[:, 2 * share_width : 3 * share_width].astype(jnp.bfloat16))
    gate_pre = projected[:, 3 * share_width :]
    forget_pre = project(normed, forget_w) + forget_bias[None, :]
    log_forget = jax.nn.log_sigmoid(forget_pre).reshape(sequences, length, heads_here)
    attended, normalizer = lax.map(
        attend_forward, (query_all, key_all, value_all, log_forget, piece_starts)
    )
    attended_flat = attended.reshape(row_count, share_width)
    gate_open = jax.nn.sigmoid(gate_pre)
    gated = (attended_flat * gate_open).astype(jnp.bfloat16)
    attention = lax.psum(contract_cols(gated, output_t).astype(jnp.bfloat16), "tensor").astype(
        jnp.float32
    )
    hidden = inputs + attention
    scale_two = lax.rsqrt(jnp.mean(hidden * hidden, axis=-1, keepdims=True) + epsilon)
    unit_two = hidden * scale_two
    normed_two = (unit_two * gain_two).astype(jnp.bfloat16)
    inner_pre = project(normed_two, gate_up_w)
    gate_part = inner_pre[:, :units]
    up_part = inner_pre[:, units:]
    inner = (jax.nn.silu(gate_part) * up_part).astype(jnp.bfloat16)
    ffn_out = lax.psum(contract_cols(inner, down_t).astype(jnp.bfloat16), "tensor").astype(
        jnp.float32
    )
    output = (hidden + ffn_out).astype(jnp.bfloat16).reshape(tokens.shape)
    upstream_low = cotangent.reshape(row_count, width)
    upstream = upstream_low.astype(jnp.float32)
    grad_down_t = contract_rows(upstream_low, inner)
    grad_inner = project(upstream_low, down_t)
    sigma = jax.nn.sigmoid(gate_part)
    grad_gate = (grad_inner * up_part * sigma * (1.0 + gate_part * (1.0 - sigma))).astype(
        jnp.bfloat16
    )
    grad_up = (grad_inner * gate_part * sigma).astype(jnp.bfloat16)
    grad_gate_up = jnp.concatenate([grad_gate, grad_up], axis=1)
    grad_gate_up_w = contract_rows(normed_two, grad_gate_up)
    grad_normed_two = lax.psum(
        contract_cols(grad_gate_up, gate_up_w).astype(jnp.bfloat16), "tensor"
    ).astype(jnp.float32)
    grad_ffn_gain = jnp.sum(grad_normed_two * unit_two, axis=0)
    ffn_sums = lax.psum_scatter(
        jnp.concatenate([grad_gate_up_w, grad_down_t, grad_ffn_gain[:, None]], axis=1).astype(
            jnp.bfloat16
        ),
        "dp",
        scatter_dimension=0,
        tiled=True,
    ).astype(jnp.float32)
    grad_unit_two = grad_normed_two * gain_two
    grad_hidden = upstream + scale_two * (
        grad_unit_two - unit_two * jnp.mean(grad_unit_two * unit_two, axis=-1, keepdims=True)
    )
    hidden_low = grad_hidden.astype(jnp.bfloat16)
    grad_output_t = contract_rows(hidden_low, gated)
    grad_gated = project(hidden_low, output_t)
    grad_attended = (grad_gated * gate_open).astype(jnp.bfloat16)
    grad_gate_pre = (grad_gated * attended_flat * gate_open * (1.0 - gate_open)).astype(
        jnp.bfloat16
    )
    grad_query, grad_key, grad_value, grad_log = lax.map(
        attend_backward,
        (
            query_all,
            key_all,
            value_all,
            log_forget,
            piece_starts,
            attended,
            normalizer,
            head_view(grad_attended),
        ),
    )
    grad_forget = (grad_log.reshape(row_count, heads_here) * jax.nn.sigmoid(-forget_pre)).astype(
        jnp.bfloat16
    )
    grad_four = jnp.concatenate(
        [
            grad_query.reshape(row_count, share_width),
            grad_key.reshape(row_count, share_width),
            grad_value.reshape(row_count, share_width),
            grad_gate_pre,
        ],
        axis=1,
    )
    grad_joined = contract_rows(normed, grad_four)
    grad_forget_w = contract_rows(normed, grad_forget)
    grad_bias = jnp.sum(grad_forget.astype(jnp.float32), axis=0)
    grad_normed = lax.psum(
        (contract_cols(grad_four, joined) + contract_cols(grad_forget, forget_w)).astype(
            jnp.bfloat16
        ),
        "tensor",
    ).astype(jnp.float32)
    grad_attn_gain = jnp.sum(grad_normed * unit_one, axis=0)
    grad_unit_one = grad_normed * gain_one
    grad_inputs = grad_hidden + scale_one * (
        grad_unit_one - unit_one * jnp.mean(grad_unit_one * unit_one, axis=-1, keepdims=True)
    )
    tokens_grad = grad_inputs.astype(jnp.bfloat16).reshape(tokens.shape)
    place = jnp.arange(width, dtype=jnp.int32) % block
    bias_col = jnp.where(
        place < heads_here, jnp.take(grad_bias, jnp.minimum(place, heads_here - 1)), 0.0
    )
    attn_sums = lax.psum_scatter(
        jnp.concatenate(
            [grad_joined, grad_output_t, grad_forget_w, grad_attn_gain[:, None], bias_col[:, None]],
            axis=1,
        ).astype(jnp.bfloat16),
        "dp",
        scatter_dimension=0,
        tiled=True,
    ).astype(jnp.float32)
    forget_at = 5 * share_width
    return (
        output,
        tokens_grad,
        attn_sums[:, forget_at + heads_here],
        attn_sums[:, :share_width],
        attn_sums[:, share_width : 2 * share_width],
        attn_sums[:, 2 * share_width : 3 * share_width],
        attn_sums[:, 3 * share_width : 4 * share_width],
        attn_sums[:, forget_at : forget_at + heads_here],
        attn_sums[:heads_here, forget_at + heads_here + 1],
        attn_sums[:, 4 * share_width : 5 * share_width].T,
        ffn_sums[:, 3 * units],
        ffn_sums[:, :units],
        ffn_sums[:, units : 2 * units],
        ffn_sums[:, 2 * units : 3 * units].T,
    )


def solution(mesh):
    placed = (
        P("dp", None, None),
        P("dp", None),
        P("dp"),
        P("dp", "tensor"),
        P("dp", "tensor"),
        P("dp", "tensor"),
        P("dp", "tensor"),
        P("dp", "tensor"),
        P("tensor"),
        P("tensor", "dp"),
        P("dp"),
        P("dp", "tensor"),
        P("dp", "tensor"),
        P("tensor", "dp"),
        P("dp", None, None),
    )
    return jax.shard_map(
        on_device,
        mesh=mesh,
        in_specs=placed,
        out_specs=(
            P("dp", None, None),
            P("dp", None, None),
            P("dp"),
            P("dp", "tensor"),
            P("dp", "tensor"),
            P("dp", "tensor"),
            P("dp", "tensor"),
            P("dp", "tensor"),
            P("tensor"),
            P("tensor", "dp"),
            P("dp"),
            P("dp", "tensor"),
            P("dp", "tensor"),
            P("tensor", "dp"),
        ),
        check_vma=False,
    )
```

profile of v0, /device:TPU:0, one launch (start us, length us, event | category | flops | bytes accessed | tf_op | source)
XLA Modules:
  0.0 1067.8 jit_solution(12600640613263816599)
XLA Ops:
  18.3 94.3 %all-gather.3.cloned.1.call-done = bf16[1536,1927]{1,0:T(8,128)(2,1)} async-done(((bf16[192,1927]{1,0:T(8,128)(2,1)}), bf16[1536,1927]{1,0:T(8,128)(2,1)}) %all-gather.3.cloned.1.call-update) | async-done | bytes 5919760 | tf_op jit(solution)/shard_map/all_gather | solution.py:169
  113.9 9.4 fusion.126
  181.1 63.7 %all-reduce.5.cloned.1.call-done = bf16[1024,1536]{1,0:T(8,128)(2,1)} async-done(((bf16[1024,1536]{1,0:T(8,128)(2,1)}), bf16[1024,1536]{1,0:T(8,128)(2,1)}) %all-reduce.5.cloned.1.call-update) | async-done | bytes 3145744 | tf_op jit(solution)/shard_map/psum | solution.py:196
  247.8 142.1 %all-gather.5.cloned.1.call-done = bf16[1536,3073]{1,0:T(8,128)(2,1)} async-done(((bf16[192,3073]{1,0:T(8,128)(2,1)}), bf16[1536,3073]{1,0:T(8,128)(2,1)}) %all-gather.5.cloned.1.call-update) | async-done | bytes 9440272 | tf_op jit(solution)/shard_map/all_gather | solution.py:175
  391.1 12.1 %fusion.43 = f32[1024,2048]{1,0:T(8,128)} fusion(bf16[1536,3073]{1,0:T(8,128)(2,1)} %all-gather.5.cloned.1.call-done, bf16[1024,1536]{1,0:T(8,128)(2,1)} %all-reduce.5.cloned.1.call-done, bf16[1,1024,1536]{2,1,0:T(8,128)(2,1)S(1)} %copy-done.1, f32[1536]{0:T(1024)S(1)} %convert_reduce_fusion, f32[1024]{0:T(1024)S(1)} %add_rsqrt_fusion), kind=kOutput, calls=%fused_computation.66 | convolution fusion | flops 6451888128 | bytes 20981760 | tf_op jit(solution)/shard_map/dot_general | solution.py:12
  403.2 8.5 fusion.47
  413.7 8.0 fusion.55
  422.5 7.6 convolution_convert_fusion.4
  430.1 58.4 %all-reduce.7.cloned.1.call-done = bf16[1024,1536]{1,0:T(8,128)(2,1)} async-done(((bf16[1024,1536]{1,0:T(8,128)(2,1)}), bf16[1024,1536]{1,0:T(8,128)(2,1)}) %all-reduce.7.cloned.1.call-update) | async-done | bytes 3145744 | tf_op jit(solution)/shard_map/psum | solution.py:222
  497.3 6.9 multiply_convert_fusion.4
  508.4 7.0 fusion.32
  517.8 9.2 subtract_multiply_fusion.1
  527.1 17.0 %fusion.11 = (f32[6,1024]{1,0:T(8,128)}, f32[6,512]{1,0:T(8,128)}, f32[6,512]{1,0:T(8,128)}, f32[6,1024]{1,0:T(8,128)}, bf16[6,512,1024]{2,1,0:T(8,128)(2,1)S(1)}) fusion(f32[6,512]{1,0:T(8,128)} %get-tuple-element.169, f32[6,1024]{1,0:T(8,128)S(1)} %bitcast.188, f32[6,512,1024]{2,1,0:T(8,128)} %subtract_multiply_fusion.1, ...), kind=kOutput, calls=%fused_computation.23 | convolution fusion | flops 446674944 | bytes 32784384 | tf_op jit(solution)/shard_map/while/body/eval_jaxpr/qhd,khd->hqk/dot_general | solution.py:99
  549.2 7.5 fusion.95
  562.2 7.2 multiply_convert_fusion.3
  593.3 9.0 fusion.51
  619.2 9.9 convolution_convert_fusion
  629.1 97.0 %all-reduce.9.cloned.1.call-done = (bf16[1024,1536]{1,0:T(8,128)(2,1)}, bf16[1024,1536]{1,0:T(8,128)(2,1)}) async-done(((bf16[1024,1536]{1,0:T(8,128)(2,1)}, bf16[1024,1536]{1,0:T(8,128)(2,1)}), (bf16[1024,1536]{1,0:T(8,128)(2,1)}, bf16[1024,1536]{1,0:T(8,128)(2,1)})) %all-reduce.9.cloned.1.call-update) | async-done | bytes 6291472 | tf_op jit(solution)/shard_map/psum | solution.py:207
  729.9 26.6 %concatenate.49 = bf16[1536,1928]{0,1:T(8,128)(2,1)} concatenate(bf16[1536,1536]{0,1:T(8,128)(2,1)} %convolution_convert_fusion, bf16[1536,384]{0,1:T(8,128)(2,1)} %convolution_convert_fusion.5, bf16[1536,6]{0,1:T(8,128)(2,1)S(1)} %copy-done.51, bf16[1536,1]{0,1:T(2,128)(2,1)S(1)} %broadcast_in_dim.195, bf16[1536,1]{0,1:T(2,128)(2,1)S(1)} %copy-done.52), dimensions={1} | concatenate | bytes 11845632 | tf_op jit(solution)/shard_map/concatenate | solution.py:290
  756.4 8.7 copy.140
  771.6 7.9 convolution_convert_fusion.1
  784.7 8.8 fusion.60
  793.6 89.9 %reduce-scatter.7.cloned.1.call-done = bf16[192,1928]{1,0:T(8,128)(2,1)} async-done(((bf16[1536,1928]{1,0:T(8,128)(2,1)}), bf16[192,1928]{1,0:T(8,128)(2,1)}) %reduce-scatter.7.cloned.1.call-update) | async-done | bytes 740368
  895.5 160.7 %reduce-scatter.5.cloned.1.call-done = bf16[192,3073]{1,0:T(8,128)(2,1)} async-done(((bf16[1536,3073]{1,0:T(8,128)(2,1)}), bf16[192,3073]{1,0:T(8,128)(2,1)}) %reduce-scatter.5.cloned.1.call-update) | async-done | bytes 1180048 | tf_op jit(solution)/shard_map/reduce_scatter | solution.py:226
  (245 shorter events, 175.0 us)
Async XLA Ops:
  7.2 106.8 %copy-start.1 = (bf16[1,1024,1536]{2,1,0:T(8,128)(2,1)S(1)}, bf16[1,1024,1536]{2,1,0:T(8,128)(2,1)}, u32[]{:S(2)}) copy-start(bf16[1,1024,1536]{2,1,0:T(8,128)(2,1)} %param.15) | copy-start | bytes 9437188
  7.2 105.4 %all-gather.3.cloned.1.call-start = ((), (), s32[]{:S(2)}) async-start(), calls=%async_computation.2 | async-start | bytes 7077888 | tf_op jit(solution)/shard_map/all_gather | solution.py:169
  11.1 233.7 %all-reduce.5.cloned.1.call-start = ((), (), s32[]{:S(2)}) async-start(), calls=%async_computation.3 | async-start | bytes 6291456 | tf_op jit(solution)/shard_map/psum | solution.py:196
  15.8 112.2 %copy-start.49 = (f32[1024]{0:T(1024)}, f32[1024]{0:T(1024)S(1)}, u32[]{:S(2)}) copy-start(f32[1024]{0:T(1024)S(1)} %add_rsqrt_fusion.1) | copy-start | bytes 12292
  113.9 14.0 %copy-start.35 = (f32[1536]{0:T(1024)}, f32[1536]{0:T(1024)S(1)}, u32[]{:S(2)}) copy-start(f32[1536]{0:T(1024)S(1)} %convert_reduce_fusion.1) | copy-start | bytes 18436
  134.5 9.5 copy-start.22
  152.9 12.6 %copy-start.16 = (f32[512,6,64]{0,2,1:T(8,128)}, f32[512,6,64]{0,2,1:T(8,128)S(1)}, u32[]{:S(2)}) copy-start(f32[512,6,64]{0,2,1:T(8,128)S(1)} %fusion.84) | copy-start | bytes 2359300
  178.0 211.9 %all-gather.5.cloned.1.call-start = ((), (), s32[]{:S(2)}) async-start(), calls=%async_computation.4 | async-start | bytes 11059200 | tf_op jit(solution)/shard_map/all_gather | solution.py:175
  181.1 307.5 %all-reduce.7.cloned.1.call-start = ((), (), s32[]{:S(2)}) async-start(), calls=%async_computation.5 | async-start | bytes 6291456 | tf_op jit(solution)/shard_map/psum | solution.py:222
  247.8 246.9 %copy-start.47 = (f32[1024]{0:T(1024)}, f32[1024]{0:T(1024)S(1)}, u32[]{:S(2)}) copy-start(f32[1024]{0:T(1024)S(1)} %add_rsqrt_fusion) | copy-start | bytes 12292
  391.1 103.6 %copy-start.37 = (f32[1536]{0:T(1024)}, f32[1536]{0:T(1024)S(1)}, u32[]{:S(2)}) copy-start(f32[1536]{0:T(1024)S(1)} %convert_reduce_fusion) | copy-start | bytes 18436
  391.1 12.1 %copy-start.20 = (bf16[1,1024,1536]{2,1,0:T(8,128)(2,1)S(1)}, bf16[1,1024,1536]{2,1,0:T(8,128)(2,1)}, u32[]{:S(2)}) copy-start(bf16[1,1024,1536]{2,1,0:T(8,128)(2,1)} %param.29) | copy-start | bytes 9437188
  391.1 12.1 %copy-start.56 = (bf16[1536,3073]{1,0:T(8,128)(2,1)S(1)}, bf16[1536,3073]{1,0:T(8,128)(2,1)}, u32[]{:S(2)}) copy-start(bf16[1536,3073]{1,0:T(8,128)(2,1)} %all-gather.5.cloned.1.call-done) | copy-start | bytes 28320772
  421.8 304.3 %all-reduce.9.cloned.1.call-start = ((), (), s32[]{:S(2)}) async-start(), calls=%async_computation.8 | async-start | bytes 12582912 | tf_op jit(solution)/shard_map/psum | solution.py:207
  517.7 9.3 copy-start.13
  527.1 17.0 %copy-start.23 = (bf16[512,384]{0,1:T(8,128)(2,1)S(1)}, bf16[512,384]{0,1:T(8,128)(2,1)}, u32[]{:S(2)}) copy-start(bf16[512,384]{0,1:T(8,128)(2,1)} %copy-done.22) | copy-start | bytes 1179652
  544.1 12.7 %slice-start = ((s8[12582912]{0:T(1024)(128)(4,1)}), s8[4194304]{0:T(1024)(128)(4,1)S(1)}, s32[]{:S(2)}) async-start(s8[12582912]{0:T(1024)(128)(4,1)} %bitcast.158), calls=%async_computation.9 | async-start | bytes 8388608
  544.1 12.7 %slice-start.1 = ((s8[12582912]{0:T(1024)(128)(4,1)}), s8[4194304]{0:T(1024)(128)(4,1)S(1)}, s32[]{:S(2)}) async-start(s8[12582912]{0:T(1024)(128)(4,1)} %bitcast.158), calls=%async_computation.10 | async-start | bytes 8388608
  562.2 9.6 copy-start.24
  562.2 12.4 %copy-start.54 = (f32[6,512]{1,0:T(8,128)S(1)}, f32[6,512]{1,0:T(8,128)}, u32[]{:S(2)}) copy-start(f32[6,512]{1,0:T(8,128)} %get-tuple-element.141) | copy-start | bytes 36868
  606.1 277.4 %reduce-scatter.7.cloned.1.call-start = ((), (), s32[]{:S(2)}) async-start(), calls=%async_computation.7 | async-start | bytes 7077888
  629.1 100.8 %copy-start.51 = (bf16[1536,6]{0,1:T(8,128)(2,1)S(1)}, bf16[1536,6]{0,1:T(8,128)(2,1)}, u32[]{:S(2)}) copy-start(bf16[1536,6]{0,1:T(8,128)(2,1)} %convolution_convert_fusion.6) | copy-start | bytes 55300
  629.1 100.8 %copy-start.52 = (bf16[1536,1]{0,1:T(2,128)(2,1)S(1)}, bf16[1536,1]{0,1:T(2,128)(2,1)}, u32[]{:S(2)}) copy-start(bf16[1536,1]{0,1:T(2,128)(2,1)} %fusion.110) | copy-start | bytes 9220
  765.1 291.0 %reduce-scatter.5.cloned.1.call-start = ((), (), s32[]{:S(2)}) async-start(), calls=%async_computation.6 | async-start | bytes 11059200 | tf_op jit(solution)/shard_map/reduce_scatter | solution.py:226
  (49 other events, 273.6 us)
Sparse Core Ops, SparseCore 0:
  11.2 101.4 all-gather.2
  178.1 66.6 all-reduce.4
  247.5 142.3 all-gather.4
  421.9 66.5 all-reduce.6
  606.3 119.7 all-reduce.8
  765.2 118.2 reduce-scatter.6
  887.1 168.9 reduce-scatter.4
where the time goes:
time: 1080 us; the launch traced here: 1070 us
  waiting for transfers between devices  706 us (65%)
  matrix products  177 us (16%)
  local copies, waits for them, and re-layouts  99 us (9%)
  other arithmetic  69.5 us (6%)
  between operations  15.2 us (1%)
    reduce_scatter x1, waiting for transfers between devices, on_device(): lax.psum_scatter(jnp.concatenate([grad_gate_up_w, grad_down_t, grad_ffn_g...  161 us
    all_gather x1, waiting for transfers between devices, on_device(): ffn_full = lax.all_gather(ffn_local, 'dp', axis=0, tiled=True)  142 us
    psum x1, waiting for transfers between devices, on_device(): lax.psum(contract_cols(inner, down_t).astype(jnp.bfloat16), 'tensor')  97 us
    all_gather x1, waiting for transfers between devices, on_device(): attn_full = lax.all_gather(attn_local, 'dp', axis=0, tiled=True)  94.3 us
    unnamed x8, waiting for transfers between devices  90.1 us
    psum x1, waiting for transfers between devices, on_device(): lax.psum(contract_cols(gated, output_t).astype(jnp.bfloat16), 'tensor')  63.7 us
    psum x1, waiting for transfers between devices, on_device(): lax.psum(contract_cols(grad_gate_up, gate_up_w).astype(jnp.bfloat16), 'te...  58.4 us
    dot_general x5, matrix products, project(): return jnp.dot(left, right, preferred_element_type=jnp.float32)  39 us
  transfers between devices with their start and end apart: 7, of which 7 were waited for; matrix products, arithmetic and copies ran while one was open for 8% of the time, Pallas kernels for 0%

commit v1 on v0

--- a/solution.py
+++ b/solution.py
@@ -166,7 +166,26 @@
     attn_local = jnp.concatenate(
         [w_query, w_key, w_value, w_outgate, w_output.T, w_forget, attn_gain[:, None]], axis=1
     )
-    attn_full = lax.all_gather(attn_local, "dp", axis=0, tiled=True)
+    count_2, index, rows = (lax.axis_size("dp"), lax.axis_index("dp"), attn_local.shape[0])
+    forward = [(i, (i + 1) % count_2) for i in range(count_2)]
+    behind = [(i, (i - 1) % count_2) for i in range(count_2)]
+    out = jnp.zeros(
+        (*attn_local.shape[:0], count_2 * rows, *attn_local.shape[0 + 1 :]), attn_local.dtype
+    )
+    out = lax.dynamic_update_slice_in_dim(out, attn_local, index * rows, axis=0)
+    from_left = from_right = attn_local
+    middle = count_2 // 2
+    for step in range(1, middle + 1):
+        from_left = lax.ppermute(from_left, "dp", forward)
+        out = lax.dynamic_update_slice_in_dim(
+            out, from_left, (index - step) % count_2 * rows, axis=0
+        )
+        if step < count_2 - middle:
+            from_right = lax.ppermute(from_right, "dp", behind)
+            out = lax.dynamic_update_slice_in_dim(
+                out, from_right, (index + step) % count_2 * rows, axis=0
+            )
+    attn_full = out
     joined = attn_full[:, : 4 * share_width]
     output_t = attn_full[:, 4 * share_width : 5 * share_width]
     forget_w = attn_full[:, 5 * share_width : 5 * share_width + heads_here]

time: 1080 us -> 1120 us (1.037)
  local copies, waits for them, and re-layouts: 99 us -> 192 us
  waiting for transfers between devices: 706 us -> 627 us
  starting transfers between devices: 0.67 us -> 20.5 us
    all_gather x1 -> x0, waiting for transfers between devices: 94.3 us -> none  [on_device(): attn_full = lax.all_gather(attn_local, 'dp', axis=0, tiled=True)]
    dynamic_update_slice x0 -> x8, local copies, waits for them, and re-layouts: none -> 86.5 us  [the longest x4 42.6 us: on_device(): lax.dynamic_update_slice_in_dim(out, from_left, (index - step) % count_2...]
    ppermute x0 -> x7, waiting for transfers between devices: none -> 84.5 us  [the longest x4 84.5 us: on_device(): from_left = lax.ppermute(from_left, 'dp', forward)]
    all_gather x1, waiting for transfers between devices: 142 us -> 73.5 us  [on_device(): ffn_full = lax.all_gather(ffn_local, 'dp', axis=0, tiled=True)]
    ppermute x0 -> x7, starting transfers between devices: none -> 19.8 us  [the longest x4 10.6 us: on_device(): from_left = lax.ppermute(from_left, 'dp', forward)]
    ppermute x0 -> x7, local copies, waits for them, and re-layouts: none -> 11.3 us  [the longest x4 6.04 us: on_device(): from_left = lax.ppermute(from_left, 'dp', forward)]
    unnamed x144 -> x160, local copies, waits for them, and re-layouts: 28 us -> 27 us
    unnamed x8 -> x7, waiting for transfers between devices: 90.1 us -> 89.9 us
  transfers between devices with their start and end apart: 7 -> 13, of which waited for: 7 -> 9; matrix products, arithmetic and copies ran while one was open for 8% -> 16% of each run, Pallas kernels for 0% -> 0%
where the time goes in v1:
time: 1120 us; the launch traced here: 1110 us
  waiting for transfers between devices  627 us (56%)
  local copies, waits for them, and re-layouts  192 us (17%)
  matrix products  183 us (16%)
  other arithmetic  69.6 us (6%)
  starting transfers between devices  20.5 us (2%)
  between operations  16.6 us (1%)
    reduce_scatter x1, waiting for transfers between devices, on_device(): lax.psum_scatter(jnp.concatenate([grad_gate_up_w, grad_down_t, grad_ffn_g...  158 us
    psum x1, waiting for transfers between devices, on_device(): lax.psum(contract_cols(inner, down_t).astype(jnp.bfloat16), 'tensor')  96.5 us
    unnamed x7, waiting for transfers between devices  89.9 us
    ppermute x4, waiting for transfers between devices, on_device(): from_left = lax.ppermute(from_left, 'dp', forward)  84.5 us
    all_gather x1, waiting for transfers between devices, on_device(): ffn_full = lax.all_gather(ffn_local, 'dp', axis=0, tiled=True)  73.5 us
    psum x1, waiting for transfers between devices, on_device(): lax.psum(contract_cols(gated, output_t).astype(jnp.bfloat16), 'tensor')  65.7 us
    psum x1, waiting for transfers between devices, on_device(): lax.psum(contract_cols(grad_gate_up, gate_up_w).astype(jnp.bfloat16), 'te...  58.4 us
    dynamic_update_slice x4, local copies, waits for them, and re-layouts, on_device(): lax.dynamic_update_slice_in_dim(out, from_left, (index - step) % count_2...  42.6 us
  transfers between devices with their start and end apart: 13, of which 9 were waited for; matrix products, arithmetic and copies ran while one was open for 16% of the time, Pallas kernels for 0%

profile of v1, /device:TPU:0, one launch (start us, length us, event | category | flops | bytes accessed | tf_op | source)
XLA Modules:
  0.0 1108.0 jit_solution(3408065705223934649)
XLA Ops:
  17.1 30.5 %collective-permute-done = bf16[192,1927]{1,0:T(8,128)(2,1)S(1)} collective-permute-done((bf16[192,1927]{1,0:T(8,128)(2,1)S(1)}, bf16[192,1927]{1,0:T(8,128)(2,1)S(1)}, u32[]{:S(2)}, u32[]{:S(2)}) %collective-permute-start) | collective-permute-done | bytes 740000 | tf_op jit(solution)/shard_map/ppermute | solution.py:179
  53.8 29.1 %collective-permute-done.2 = bf16[192,1927]{1,0:T(8,128)(2,1)S(1)} collective-permute-done((bf16[192,1927]{1,0:T(8,128)(2,1)S(1)}, bf16[192,1927]{1,0:T(8,128)(2,1)S(1)}, u32[]{:S(2)}, u32[]{:S(2)}) %collective-permute-start.2) | collective-permute-done | bytes 740000 | tf_op jit(solution)/shard_map/ppermute | solution.py:179
  92.5 24.9 %collective-permute-done.4 = bf16[192,1927]{1,0:T(8,128)(2,1)} collective-permute-done((bf16[192,1927]{1,0:T(8,128)(2,1)S(1)}, bf16[192,1927]{1,0:T(8,128)(2,1)}, u32[]{:S(2)}, u32[]{:S(2)}) %collective-permute-start.4) | collective-permute-done | bytes 740000 | tf_op jit(solution)/shard_map/ppermute | solution.py:179
  123.8 10.2 dynamic_update_slice.40
  137.3 10.6 dynamic_update_slice.41
  148.7 11.3 %dynamic_update_slice.42 = bf16[1536,1927]{0,1:T(8,128)(2,1)} dynamic-update-slice(bf16[1536,1927]{0,1:T(8,128)(2,1)} %dynamic_update_slice.41, bf16[192,1927]{0,1:T(8,128)(2,1)S(1)} %copy.132, s32[]{:T(128)S(6)} %select_n.151, s32[]{:T(128)} %constant.170.clone.1) | dynamic-update-slice | bytes 1479940 | tf_op jit(solution)/shard_map/dynamic_update_slice | solution.py:185
  160.9 9.8 dynamic_update_slice.43
  172.9 10.6 dynamic_update_slice.44
  185.7 11.8 %dynamic_update_slice.45 = bf16[1536,1927]{0,1:T(8,128)(2,1)} dynamic-update-slice(bf16[1536,1927]{0,1:T(8,128)(2,1)} %dynamic_update_slice.44, bf16[192,1927]{0,1:T(8,128)(2,1)} %copy.135, s32[]{:T(128)S(6)} %select_n.157, s32[]{:T(128)} %constant.170.clone.1) | dynamic-update-slice | bytes 1479940 | tf_op jit(solution)/shard_map/dynamic_update_slice | solution.py:180
  199.7 11.8 %dynamic_update_slice.46 = bf16[1536,1927]{0,1:T(8,128)(2,1)} dynamic-update-slice(bf16[1536,1927]{0,1:T(8,128)(2,1)} %dynamic_update_slice.45, bf16[192,1927]{0,1:T(8,128)(2,1)} %copy.136, s32[]{:T(128)S(6)} %select_n.159, s32[]{:T(128)} %constant.170.clone.1) | dynamic-update-slice | bytes 1479940 | tf_op jit(solution)/shard_map/dynamic_update_slice | solution.py:185
  213.7 10.4 dynamic_update_slice.47
  224.9 9.5 fusion.127
  295.3 65.7 %all-reduce.5.cloned.1.call-done = bf16[1024,1536]{1,0:T(8,128)(2,1)} async-done(((bf16[1024,1536]{1,0:T(8,128)(2,1)}), bf16[1024,1536]{1,0:T(8,128)(2,1)}) %all-reduce.5.cloned.1.call-update) | async-done | bytes 3145744 | tf_op jit(solution)/shard_map/psum | solution.py:215
  364.0 73.5 %all-gather.2.cloned.1.call-done = bf16[1536,3073]{1,0:T(8,128)(2,1)} async-done(((bf16[192,3073]{1,0:T(8,128)(2,1)}), bf16[1536,3073]{1,0:T(8,128)(2,1)}) %all-gather.2.cloned.1.call-update) | async-done | bytes 9440272 | tf_op jit(solution)/shard_map/all_gather | solution.py:194
  438.8 12.0 %fusion.43 = f32[1024,2048]{1,0:T(8,128)} fusion(bf16[1536,3073]{1,0:T(8,128)(2,1)} %all-gather.2.cloned.1.call-done, bf16[1024,1536]{1,0:T(8,128)(2,1)} %all-reduce.5.cloned.1.call-done, bf16[1,1024,1536]{2,1,0:T(8,128)(2,1)S(1)} %copy-done.2, f32[1536]{0:T(1024)S(1)} %convert_reduce_fusion, f32[1024]{0:T(1024)S(1)} %add_rsqrt_fusion), kind=kOutput, calls=%fused_computation.66 | convolution fusion | flops 6451888128 | bytes 20981760 | tf_op jit(solution)/shard_map/dot_general | solution.py:12
  477.7 58.4 %all-reduce.7.cloned.1.call-done = bf16[1024,1536]{1,0:T(8,128)(2,1)} async-done(((bf16[1024,1536]{1,0:T(8,128)(2,1)}), bf16[1024,1536]{1,0:T(8,128)(2,1)}) %all-reduce.7.cloned.1.call-update) | async-done | bytes 3145744 | tf_op jit(solution)/shard_map/psum | solution.py:241
  566.8 8.9 subtract_multiply_fusion.1
  575.8 18.1 %fusion.11 = (f32[6,1024]{1,0:T(8,128)}, f32[6,512]{1,0:T(8,128)}, f32[6,512]{1,0:T(8,128)}, f32[6,1024]{1,0:T(8,128)}, bf16[6,512,1024]{2,1,0:T(8,128)(2,1)}) fusion(f32[6,512]{1,0:T(8,128)S(1)} %copy-done.62, f32[6,1024]{1,0:T(8,128)S(1)} %bitcast.188, f32[6,512,1024]{2,1,0:T(8,128)} %subtract_multiply_fusion.1, f32[6,512]{1,0:T(8,128)S(1)} %copy-done.61, ...), kind=kOutput, calls=%fused_computation.23 | convolution fusion | flops 446674944 | bytes 32784384 | tf_op jit(solution)/shard_map/while/body/eval_jaxpr/qhd,khd->hqk/dot_general | solution.py:99
  637.2 11.1 %add_convert_fusion = bf16[1024,1536]{1,0:T(8,128)(2,1)} fusion(f32[1024,1536]{1,0:T(8,128)S(1)} %fusion.106, bf16[1536,1927]{0,1:T(8,128)(2,1)} %dynamic_update_slice.47, bf16[1024,384]{1,0:T(8,128)(2,1)S(1)} %copy-done.65, bf16[1024,384]{1,0:T(8,128)(2,1)S(1)} %copy-done.26, bf16[1024,384]{1,0:T(8,128)(2,1)S(1)} %copy-done.28, ...), kind=kOutput, calls=%fused_computation.55 | convolution fusion | flops 4850712576 | bytes 17301504 | tf_op jit(solution)/shard_map/dot_general | solution.py:22
  661.8 9.9 convolution_convert_fusion
  671.7 96.5 %all-reduce.9.cloned.1.call-done = (bf16[1024,1536]{1,0:T(8,128)(2,1)}, bf16[1024,1536]{1,0:T(8,128)(2,1)}) async-done(((bf16[1024,1536]{1,0:T(8,128)(2,1)}, bf16[1024,1536]{1,0:T(8,128)(2,1)}), (bf16[1024,1536]{1,0:T(8,128)(2,1)}, bf16[1024,1536]{1,0:T(8,128)(2,1)})) %all-reduce.9.cloned.1.call-update) | async-done | bytes 6291472 | tf_op jit(solution)/shard_map/psum | solution.py:226
  772.1 26.6 %concatenate.49 = bf16[1536,1928]{0,1:T(8,128)(2,1)} concatenate(bf16[1536,1536]{0,1:T(8,128)(2,1)} %convolution_convert_fusion, bf16[1536,384]{0,1:T(8,128)(2,1)} %convolution_convert_fusion.5, bf16[1536,6]{0,1:T(8,128)(2,1)S(1)} %copy-done.57, bf16[1536,1]{0,1:T(2,128)(2,1)S(1)} %broadcast_in_dim.199, bf16[1536,1]{0,1:T(2,128)(2,1)S(1)} %copy-done.58), dimensions={1} | concatenate | bytes 11845632 | tf_op jit(solution)/shard_map/concatenate | solution.py:309
  835.8 89.8 %reduce-scatter.7.cloned.1.call-done = bf16[192,1928]{1,0:T(8,128)(2,1)} async-done(((bf16[1536,1928]{1,0:T(8,128)(2,1)}), bf16[192,1928]{1,0:T(8,128)(2,1)}) %reduce-scatter.7.cloned.1.call-update) | async-done | bytes 740368
  937.6 158.4 %reduce-scatter.5.cloned.1.call-done = bf16[192,3073]{1,0:T(8,128)(2,1)} async-done(((bf16[1536,3073]{1,0:T(8,128)(2,1)}), bf16[192,3073]{1,0:T(8,128)(2,1)}) %reduce-scatter.5.cloned.1.call-update) | async-done | bytes 1180048 | tf_op jit(solution)/shard_map/reduce_scatter | solution.py:245
  (289 shorter events, 281.7 us)
Async XLA Ops:
  8.0 353.0 %all-reduce.5.cloned.1.call-start = ((), (), s32[]{:S(2)}) async-start(), calls=%async_computation.2 | async-start | bytes 6291456 | tf_op jit(solution)/shard_map/psum | solution.py:215
  11.0 36.7 %collective-permute-start = (bf16[192,1927]{1,0:T(8,128)(2,1)S(1)}, bf16[192,1927]{1,0:T(8,128)(2,1)S(1)}, u32[]{:S(2)}, u32[]{:S(2)}) collective-permute-start(bf16[192,1927]{1,0:T(8,128)(2,1)S(1)} %concatenate.40), channel_id=1, source_target_pairs={{0,4},{4,8},{8,12},{12,16},{16,20},{20,24},{24,28},{28,0},{1,5},{5... | collective-permute-start | bytes 2219912 | tf_op jit(solution)/shard_map/ppermute | solution.py:179
  14.0 36.8 %collective-permute-start.1 = (bf16[192,1927]{1,0:T(8,128)(2,1)S(1)}, bf16[192,1927]{1,0:T(8,128)(2,1)S(1)}, u32[]{:S(2)}, u32[]{:S(2)}) collective-permute-start(bf16[192,1927]{1,0:T(8,128)(2,1)S(1)} %concatenate.40), channel_id=1, source_target_pairs={{0,28},{4,0},{8,4},{12,8},{16,12},{20,16},{24,20},{28,24},{1,29},{... | collective-permute-start | bytes 2219912 | tf_op jit(solution)/shard_map/ppermute | solution.py:184
  47.7 35.3 %copy-start.24 = (bf16[192,1927]{1,0:T(8,128)(2,1)}, bf16[192,1927]{1,0:T(8,128)(2,1)S(1)}, u32[]{:S(2)}) copy-start(bf16[192,1927]{1,0:T(8,128)(2,1)S(1)} %collective-permute-done) | copy-start | bytes 2219908
  47.7 35.3 %collective-permute-start.2 = (bf16[192,1927]{1,0:T(8,128)(2,1)S(1)}, bf16[192,1927]{1,0:T(8,128)(2,1)S(1)}, u32[]{:S(2)}, u32[]{:S(2)}) collective-permute-start(bf16[192,1927]{1,0:T(8,128)(2,1)S(1)} %collective-permute-done), channel_id=1, source_target_pairs={{0,4},{4,8},{8,12},{12,16},{16,20},{20,24},{24,28},{28,0},{1,5},{5... | collective-permute-start | bytes 2219912 | tf_op jit(solution)/shard_map/ppermute | solution.py:179
  50.8 38.6 %collective-permute-start.3 = (bf16[192,1927]{1,0:T(8,128)(2,1)S(1)}, bf16[192,1927]{1,0:T(8,128)(2,1)}, u32[]{:S(2)}, u32[]{:S(2)}) collective-permute-start(bf16[192,1927]{1,0:T(8,128)(2,1)S(1)} %collective-permute-done.1), channel_id=1, source_target_pairs={{0,28},{4,0},{8,4},{12,8},{16,12},{20,16},{24,20},{28,24},{1,29},{... | collective-permute-start | bytes 2219912 | tf_op jit(solution)/shard_map/ppermute | solution.py:184
  82.9 34.5 %collective-permute-start.4 = (bf16[192,1927]{1,0:T(8,128)(2,1)S(1)}, bf16[192,1927]{1,0:T(8,128)(2,1)}, u32[]{:S(2)}, u32[]{:S(2)}) collective-permute-start(bf16[192,1927]{1,0:T(8,128)(2,1)S(1)} %collective-permute-done.2), channel_id=1, source_target_pairs={{0,4},{4,8},{8,12},{12,16},{16,20},{20,24},{24,28},{28,0},{1,5},{5... | collective-permute-start | bytes 2219912 | tf_op jit(solution)/shard_map/ppermute | solution.py:179
  89.4 147.1 %copy-start.54 = (f32[1024]{0:T(1024)}, f32[1024]{0:T(1024)S(1)}, u32[]{:S(2)}) copy-start(f32[1024]{0:T(1024)S(1)} %add_rsqrt_fusion.1) | copy-start | bytes 12292
  89.4 108.1 %collective-permute-start.5 = (bf16[192,1927]{1,0:T(8,128)(2,1)}, bf16[192,1927]{1,0:T(8,128)(2,1)}, u32[]{:S(2)}, u32[]{:S(2)}) collective-permute-start(bf16[192,1927]{1,0:T(8,128)(2,1)} %collective-permute-done.3), channel_id=1, source_target_pairs={{0,28},{4,0},{8,4},{12,8},{16,12},{20,16},{24,20},{28,24},{1,29},{... | collective-permute-start | bytes 2219912 | tf_op jit(solution)/shard_map/ppermute | solution.py:184
  117.4 94.1 %collective-permute-start.6 = (bf16[192,1927]{1,0:T(8,128)(2,1)}, bf16[192,1927]{1,0:T(8,128)(2,1)}, u32[]{:S(2)}, u32[]{:S(2)}) collective-permute-start(bf16[192,1927]{1,0:T(8,128)(2,1)} %collective-permute-done.4), channel_id=1, source_target_pairs={{0,4},{4,8},{8,12},{12,16},{16,20},{20,24},{24,28},{28,0},{1,5},{5... | collective-permute-start | bytes 2219912 | tf_op jit(solution)/shard_map/ppermute | solution.py:179
  120.8 15.6 %copy-start.25 = (bf16[192,1927]{1,0:T(8,128)(2,1)S(1)}, bf16[192,1927]{1,0:T(8,128)(2,1)}, u32[]{:S(2)}) copy-start(bf16[192,1927]{1,0:T(8,128)(2,1)} %copy-done.24) | copy-start | bytes 2219908
  172.9 51.9 %copy-start.2 = (bf16[1,1024,1536]{2,1,0:T(8,128)(2,1)S(1)}, bf16[1,1024,1536]{2,1,0:T(8,128)(2,1)}, u32[]{:S(2)}) copy-start(bf16[1,1024,1536]{2,1,0:T(8,128)(2,1)} %param.15) | copy-start | bytes 9437188
  267.0 12.7 %copy-start.14 = (f32[512,6,64]{0,2,1:T(8,128)}, f32[512,6,64]{0,2,1:T(8,128)S(1)}, u32[]{:S(2)}) copy-start(f32[512,6,64]{0,2,1:T(8,128)S(1)} %fusion.83) | copy-start | bytes 2359300
  292.2 145.4 %all-gather.2.cloned.1.call-start = ((), (), s32[]{:S(2)}) async-start(), calls=%async_computation.3 | async-start | bytes 11059200 | tf_op jit(solution)/shard_map/all_gather | solution.py:194
  295.2 240.9 %all-reduce.7.cloned.1.call-start = ((), (), s32[]{:S(2)}) async-start(), calls=%async_computation.4 | async-start | bytes 6291456 | tf_op jit(solution)/shard_map/psum | solution.py:241
  364.0 177.9 %copy-start.52 = (f32[1024]{0:T(1024)}, f32[1024]{0:T(1024)S(1)}, u32[]{:S(2)}) copy-start(f32[1024]{0:T(1024)S(1)} %add_rsqrt_fusion) | copy-start | bytes 12292
  438.8 103.2 %copy-start.41 = (f32[1536]{0:T(1024)}, f32[1536]{0:T(1024)S(1)}, u32[]{:S(2)}) copy-start(f32[1536]{0:T(1024)S(1)} %convert_reduce_fusion) | copy-start | bytes 18436
  438.8 12.0 %copy-start.18 = (bf16[1,1024,1536]{2,1,0:T(8,128)(2,1)S(1)}, bf16[1,1024,1536]{2,1,0:T(8,128)(2,1)}, u32[]{:S(2)}) copy-start(bf16[1,1024,1536]{2,1,0:T(8,128)(2,1)} %param.29) | copy-start | bytes 9437188
  469.3 298.9 %all-reduce.9.cloned.1.call-start = ((), (), s32[]{:S(2)}) async-start(), calls=%async_computation.7 | async-start | bytes 12582912 | tf_op jit(solution)/shard_map/psum | solution.py:226
  622.9 12.4 %copy-start.50 = (bf16[1024,6]{0,1:T(8,128)(2,1)}, bf16[1024,6]{0,1:T(8,128)(2,1)S(1)}, u32[]{:S(2)}) copy-start(bf16[1024,6]{0,1:T(8,128)(2,1)S(1)} %get-tuple-element.146) | copy-start | bytes 36868
  648.4 277.2 %reduce-scatter.7.cloned.1.call-start = ((), (), s32[]{:S(2)}) async-start(), calls=%async_computation.6 | async-start | bytes 7077888
  671.7 100.3 %copy-start.57 = (bf16[1536,6]{0,1:T(8,128)(2,1)S(1)}, bf16[1536,6]{0,1:T(8,128)(2,1)}, u32[]{:S(2)}) copy-start(bf16[1536,6]{0,1:T(8,128)(2,1)} %convolution_convert_fusion.6) | copy-start | bytes 55300
  671.7 100.3 %copy-start.58 = (bf16[1536,1]{0,1:T(2,128)(2,1)S(1)}, bf16[1536,1]{0,1:T(2,128)(2,1)}, u32[]{:S(2)}) copy-start(bf16[1536,1]{0,1:T(2,128)(2,1)} %fusion.111) | copy-start | bytes 9220
  807.4 288.5 %reduce-scatter.5.cloned.1.call-start = ((), (), s32[]{:S(2)}) async-start(), calls=%async_computation.5 | async-start | bytes 11059200 | tf_op jit(solution)/shard_map/reduce_scatter | solution.py:245
  (63 other events, 362.2 us)
Sparse Core Ops, SparseCore 0:
  292.3 68.6 all-reduce.4
  469.5 66.5 all-reduce.6
  648.5 119.6 all-reduce.8
Sparse Core Ops, SparseCore 1:
  295.4 142.1 all-gather.1
  807.5 118.1 reduce-scatter.6
  929.1 166.8 reduce-scatter.4
